TPU v7x, 512 devices: a whole 4x4x16 slice. The times are simulated.
512 devices in a mesh: blk: 32 (over z, y_lo), rep: 16 (over x, y_hi, core).
Axes of the slice: x: 4, y: 4 (y_hi: 2, y_lo: 2; y = y_hi * 2 + y_lo), z: 16, core: 2. Of those that a mesh axis runs over, the one named last changes fastest.
Arguments:
- feats: bfloat16 [32768, 256], P(('blk', 'rep')), may hold values from -6 to 6
- weight: bfloat16 [256, 256], replicated, may hold values from -0.375 to 0.375
- bias: float32 [256], replicated, may hold values from -4 to 4
- grad_out: bfloat16 [32768, 256], P(('blk', 'rep')), may hold values from -6 to 6
- tile_values: bfloat16 [32, 16, 2, 64, 128, 128], P('blk', 'rep'), may hold values from -0.03125 to 0.03125
- tile_rows: int32 [32, 16, 2, 64], P('blk', 'rep'), may hold values from 0 to 7, as said below
- tile_cols: int32 [32, 16, 2, 64], P('blk', 'rep'), may hold values from 0 to 7, as said below
- tile_count: int32 [32, 16, 2], P('blk', 'rep'), may hold values from 32 to 64, as said below
Outputs:
- out: bfloat16 [32768, 256], P(('blk', 'rep'))
- grad_feats: bfloat16 [32768, 256], P(('blk', 'rep'))
- grad_weight: float32 [256, 256], P('rep')
- grad_bias: float32 [256], replicated
Inputs may be any that keep to these rules, and one draw needn't show every extreme that they name: `tile_count`: some pair slot of some device holds exactly 64 live entries; slots past the count hold values that must be ignored. Within one pair slot the 64 entries name distinct (tile_rows, tile_cols) cells. `tile_cols`: see tile_rows: cells of one slot are distinct.
All inputs are finite; a program needn't handle non-finite values.
Results may differ from a plain program's by a relative error of at most 0.018.
Values may be sent and summed in bfloat16 or wider, within the bound.
No kernel may reach another device: no remote copies, remote signals or barrier semaphores. Data moves between devices by JAX's collectives and lax.ppermute only.
A program may use at most 64 MiB of HBM per device.

v0:
```python
import jax
import jax.numpy as jnp
from jax import lax
from jax.sharding import PartitionSpec as P


def passed_along(x, axis, by):
    devices = lax.axis_size(axis)
    return lax.ppermute(x, axis, [(i, (i + by) % devices) for i in range(devices)])


def dense_adjacency(tile_vals, tile_row, tile_col, live, tiles_per_part):
    entries, tile_size, _ = tile_vals.shape
    cells = tiles_per_part * tiles_per_part
    cell_of_entry = tile_row * tiles_per_part + tile_col
    alive = jnp.arange(entries) < live
    select = (cell_of_entry[None, :] == jnp.arange(cells)[:, None]) & alive[None, :]
    placed = jnp.dot(
        select.astype(tile_vals.dtype),
        tile_vals.reshape(entries, tile_size * tile_size),
        preferred_element_type=jnp.float32,
    ).astype(tile_vals.dtype)
    placed = placed.reshape(tiles_per_part, tiles_per_part, tile_size, tile_size)
    side = tiles_per_part * tile_size
    return placed.transpose(0, 2, 1, 3).reshape(side, side)


def activation(pre_act, cotangent):
    logistic = jax.nn.sigmoid(pre_act)
    result = (pre_act * logistic).astype(jnp.bfloat16)
    grad_pre = (
        cotangent.astype(jnp.float32) * logistic * (1.0 + pre_act * (1.0 - logistic))
    ).astype(jnp.bfloat16)
    return (result, grad_pre)


def body(feats, weight, bias, grad_out, tile_values, tile_rows, tile_cols, tile_count):
    replicas = lax.axis_size("rep")
    rep_index = lax.axis_index("rep")
    tile_size = tile_values.shape[-1]
    pair_slots = tile_values.shape[2]
    digit_count = (replicas - 1).bit_length()
    values_here = tile_values[0, 0]
    rows_here = tile_rows[0, 0]
    cols_here = tile_cols[0, 0]
    counts_here = tile_count[0, 0]
    hw_slice = jnp.dot(feats, weight, preferred_element_type=jnp.float32).astype(jnp.bfloat16)
    feature_block = lax.all_gather(hw_slice, "rep", axis=0, tiled=True)
    for level in range(digit_count):
        shifted = passed_along(feature_block, "blk", 1 << level)
        feature_block = jnp.where(rep_index // (1 << level) % 2 == 1, shifted, feature_block)
    tiles_per_part = feature_block.shape[0] // tile_size
    adjacency = [
        dense_adjacency(
            values_here[slot], rows_here[slot], cols_here[slot], counts_here[slot], tiles_per_part
        )
        for slot in range(pair_slots)
    ]
    aggregate = jnp.zeros(feature_block.shape, jnp.float32)
    for slot in range(pair_slots):
        aggregate = aggregate + jnp.dot(
            adjacency[slot], feature_block, preferred_element_type=jnp.float32
        )
        if slot + 1 < pair_slots:
            feature_block = passed_along(feature_block, "blk", replicas)
    aggregate_rows = lax.psum_scatter(
        aggregate.astype(jnp.bfloat16), "rep", scatter_dimension=0, tiled=True
    ).astype(jnp.float32)
    out, grad_rows = activation(aggregate_rows + bias, grad_out)
    grad_block = lax.all_gather(grad_rows, "rep", axis=0, tiled=True)
    partial_grad = jnp.zeros(grad_block.shape, jnp.float32)
    for slot in reversed(range(pair_slots)):
        partial_grad = partial_grad + lax.dot_general(
            adjacency[slot],
            grad_block,
            (((0,), (0,)), ((), ())),
            preferred_element_type=jnp.float32,
        )
        if slot > 0:
            partial_grad = passed_along(partial_grad.astype(jnp.bfloat16), "blk", -replicas).astype(
                partial_grad.dtype
            )
    for level in reversed(range(digit_count)):
        shifted = passed_along(partial_grad.astype(jnp.bfloat16), "blk", -(1 << level)).astype(
            partial_grad.dtype
        )
        partial_grad = jnp.where(rep_index // (1 << level) % 2 == 1, shifted, partial_grad)
    grad_hw = lax.psum_scatter(
        partial_grad.astype(jnp.bfloat16), "rep", scatter_dimension=0, tiled=True
    )
    grad_feats = lax.dot_general(
        grad_hw, weight, (((1,), (1,)), ((), ())), preferred_element_type=jnp.float32
    ).astype(jnp.bfloat16)
    weight_terms = lax.dot_general(
        feats, grad_hw, (((0,), (0,)), ((), ())), preferred_element_type=jnp.float32
    )
    weight_rows = weight.shape[0] // replicas
    bias_terms = jnp.sum(grad_rows.astype(jnp.float32), axis=0)
    weight_total, grad_bias = lax.psum((weight_terms, bias_terms), ("blk", "rep"))
    grad_weight = lax.dynamic_slice_in_dim(weight_total, rep_index * weight_rows, weight_rows, 0)
    return (out, grad_feats, grad_weight, grad_bias)


def solution(mesh):
    in_specs = (
        P(("blk", "rep"), None),
        P(),
        P(),
        P(("blk", "rep"), None),
        P("blk", "rep", None, None, None, None),
        P("blk", "rep", None, None),
        P("blk", "rep", None, None),
        P("blk", "rep", None),
    )
    out_specs = (P(("blk", "rep"), None), P(("blk", "rep"), None), P("rep", None), P())
    return jax.shard_map(body, mesh=mesh, in_specs=in_specs, out_specs=out_specs, check_vma=False)
```

profile of v0, /device:TPU:4, one launch (start us, length us, event | category | flops | bytes accessed | tf_op | source)
XLA Modules:
  0.0 1048.3 jit_solution(11181954026101608006)
XLA Ops:
  7.2 0.8 copy-done
  8.1 0.9 convolution_convert_fusion.3
  9.0 22.4 %all_gather.6 = bf16[1024,256]{1,0:T(8,128)(2,1)S(1)} all-gather(bf16[64,256]{1,0:T(8,128)(2,1)S(1)} %convolution_convert_fusion.3), channel_id=1, replica_groups=mesh['blk'=32,'rep'=16] {'rep'}, dimensions={0}, use_global_device_ids=true | all-gather | bytes 557056 | tf_op jit(solution)/shard_map/all_gather | solution.py:48
  31.4 2.1 collective-permute-start
  33.5 21.3 %collective-permute-done = bf16[1024,256]{1,0:T(8,128)(2,1)S(1)} collective-permute-done((bf16[1024,256]{1,0:T(8,128)(2,1)S(1)}, bf16[1024,256]{1,0:T(8,128)(2,1)S(1)}, u32[]{:S(2)}, u32[]{:S(2)}) %collective-permute-start) | collective-permute-done | bytes 524320 | tf_op jit(solution)/shard_map/ppermute | solution.py:9
  54.8 0.1 broadcast_select_fusion
  54.9 1.9 collective-permute-start.1
  56.9 14.7 %collective-permute-done.1 = bf16[1024,256]{1,0:T(8,128)(2,1)S(1)} collective-permute-done((bf16[1024,256]{1,0:T(8,128)(2,1)S(1)}, bf16[1024,256]{1,0:T(8,128)(2,1)S(1)}, u32[]{:S(2)}, u32[]{:S(2)}) %collective-permute-start.1) | collective-permute-done | bytes 524320 | tf_op jit(solution)/shard_map/ppermute | solution.py:9
  71.7 1.9 collective-permute-start.2
  73.7 25.6 %collective-permute-done.2 = bf16[1024,256]{1,0:T(8,128)(2,1)S(1)} collective-permute-done((bf16[1024,256]{1,0:T(8,128)(2,1)S(1)}, bf16[1024,256]{1,0:T(8,128)(2,1)S(1)}, u32[]{:S(2)}, u32[]{:S(2)}) %collective-permute-start.2) | collective-permute-done | bytes 524320 | tf_op jit(solution)/shard_map/ppermute | solution.py:9
  99.4 2.4 collective-permute-start.3
  101.8 0.6 fusion.37
  102.4 0.6 iota_compare_fusion.3
  103.0 2.7 fusion.36
  105.7 41.7 %collective-permute-done.3 = bf16[1024,256]{1,0:T(8,128)(2,1)S(1)} collective-permute-done((bf16[1024,256]{1,0:T(8,128)(2,1)S(1)}, bf16[1024,256]{1,0:T(8,128)(2,1)S(1)}, u32[]{:S(2)}, u32[]{:S(2)}) %collective-permute-start.3) | collective-permute-done | bytes 524320 | tf_op jit(solution)/shard_map/ppermute | solution.py:9
  147.4 0.1 broadcast_select_fusion.3
  147.5 5.2 collective-permute-start.4
  152.7 1.7 convolution_convert_fusion.1
  154.4 0.7 iota_compare_fusion.2
  155.0 1.7 convolution_convert_fusion
  156.7 24.6 %collective-permute-done.4 = bf16[1024,256]{1,0:T(8,128)(2,1)S(1)} collective-permute-done((bf16[1024,256]{1,0:T(8,128)(2,1)S(1)}, bf16[1024,256]{1,0:T(8,128)(2,1)S(1)}, u32[]{:S(2)}, u32[]{:S(2)}) %collective-permute-start.4) | collective-permute-done | bytes 524320 | tf_op jit(solution)/shard_map/ppermute | solution.py:9
  181.4 0.7 fusion.2
  182.1 1.5 fusion.22
  183.7 109.7 %reduce-scatter.3.cloned.1.call-done = bf16[64,256]{1,0:T(8,128)(2,1)} async-done(((bf16[1024,256]{1,0:T(8,128)(2,1)}), bf16[64,256]{1,0:T(8,128)(2,1)}) %reduce-scatter.3.cloned.1.call-update) | async-done | bytes 32784 | tf_op jit(solution)/shard_map/reduce_scatter | solution.py:66
  293.4 1.4 convert_reduce_fusion
  294.9 21.4 %all_gather.7 = bf16[1024,256]{1,0:T(8,128)(2,1)S(1)} all-gather(bf16[64,256]{1,0:T(8,128)(2,1)S(1)} %get-tuple-element.9), channel_id=1, replica_groups=mesh['blk'=32,'rep'=16] {'rep'}, dimensions={0}, use_global_device_ids=true | all-gather | bytes 557056 | tf_op jit(solution)/shard_map/all_gather | solution.py:70
  316.3 2.4 fusion.19
  318.7 12.8 %collective-permute-start.5 = (bf16[1024,256]{1,0:T(8,128)(2,1)S(1)}, bf16[1024,256]{1,0:T(8,128)(2,1)S(1)}, u32[]{:S(2)}, u32[]{:S(2)}) collective-permute-start(bf16[1024,256]{1,0:T(8,128)(2,1)S(1)} %fusion.19), channel_id=1, source_target_pairs={{0,256},{16,272},{32,288},{48,304},{64,320},{80,336},{96,352},{112... | collective-permute-start | bytes 1572872 | tf_op jit(solution)/shard_map/ppermute | solution.py:9
  331.5 25.8 %collective-permute-done.5 = bf16[1024,256]{1,0:T(8,128)(2,1)S(1)} collective-permute-done((bf16[1024,256]{1,0:T(8,128)(2,1)S(1)}, bf16[1024,256]{1,0:T(8,128)(2,1)S(1)}, u32[]{:S(2)}, u32[]{:S(2)}) %collective-permute-start.5) | collective-permute-done | bytes 524320 | tf_op jit(solution)/shard_map/ppermute | solution.py:9
  357.3 0.8 fusion.25
  358.0 17.0 %collective-permute-start.6 = (bf16[1024,256]{1,0:T(8,128)(2,1)S(1)}, bf16[1024,256]{1,0:T(8,128)(2,1)S(1)}, u32[]{:S(2)}, u32[]{:S(2)}) collective-permute-start(bf16[1024,256]{1,0:T(8,128)(2,1)S(1)} %get-tuple-element.17), channel_id=1, source_target_pairs={{0,384},{16,400},{32,416},{48,432},{64,448},{80,464},{96,480},{112... | collective-permute-start | bytes 1572872 | tf_op jit(solution)/shard_map/ppermute | solution.py:9
  375.0 23.2 %collective-permute-done.6 = bf16[1024,256]{1,0:T(8,128)(2,1)S(1)} collective-permute-done((bf16[1024,256]{1,0:T(8,128)(2,1)S(1)}, bf16[1024,256]{1,0:T(8,128)(2,1)S(1)}, u32[]{:S(2)}, u32[]{:S(2)}) %collective-permute-start.6) | collective-permute-done | bytes 524320 | tf_op jit(solution)/shard_map/ppermute | solution.py:9
  398.2 0.2 convert_select_fusion.2
  398.4 25.2 %collective-permute-start.7 = (bf16[1024,256]{1,0:T(8,128)(2,1)S(1)}, bf16[1024,256]{1,0:T(8,128)(2,1)S(1)}, u32[]{:S(2)}, u32[]{:S(2)}) collective-permute-start(bf16[1024,256]{1,0:T(8,128)(2,1)S(1)} %convert_select_fusion.2), channel_id=1, source_target_pairs={{0,448},{16,464},{32,480},{48,496},{64,0},{80,16},{96,32},{112,48}... | collective-permute-start | bytes 1572872 | tf_op jit(solution)/shard_map/ppermute | solution.py:9
  423.7 26.4 %collective-permute-done.7 = bf16[1024,256]{1,0:T(8,128)(2,1)S(1)} collective-permute-done((bf16[1024,256]{1,0:T(8,128)(2,1)S(1)}, bf16[1024,256]{1,0:T(8,128)(2,1)S(1)}, u32[]{:S(2)}, u32[]{:S(2)}) %collective-permute-start.7) | collective-permute-done | bytes 524320 | tf_op jit(solution)/shard_map/ppermute | solution.py:9
  450.0 0.1 fusion.26
  450.2 1.9 collective-permute-start.8
  452.1 13.8 %collective-permute-done.8 = bf16[1024,256]{1,0:T(8,128)(2,1)S(1)} collective-permute-done((bf16[1024,256]{1,0:T(8,128)(2,1)S(1)}, bf16[1024,256]{1,0:T(8,128)(2,1)S(1)}, u32[]{:S(2)}, u32[]{:S(2)}) %collective-permute-start.8) | collective-permute-done | bytes 524320 | tf_op jit(solution)/shard_map/ppermute | solution.py:9
  465.9 0.2 fusion.27
  466.1 3.5 collective-permute-start.9
  469.6 11.4 %collective-permute-done.9 = bf16[1024,256]{1,0:T(8,128)(2,1)S(1)} collective-permute-done((bf16[1024,256]{1,0:T(8,128)(2,1)S(1)}, bf16[1024,256]{1,0:T(8,128)(2,1)S(1)}, u32[]{:S(2)}, u32[]{:S(2)}) %collective-permute-start.9) | collective-permute-done | bytes 524320 | tf_op jit(solution)/shard_map/ppermute | solution.py:9
  481.0 1.0 select_convert_fusion
  482.1 106.1 %psum.15 = f32[256]{0:T(256)} all-reduce(f32[256]{0:T(256)S(1)} %get-tuple-element.8), channel_id=1, replica_groups=mesh['blk'=32,'rep'=16] {'blk','rep'}, use_global_device_ids=true, to_apply=%region_4.5 | all-reduce | flops 256 | bytes 2048 | tf_op jit(solution)/shard_map/psum | solution.py:99
  588.2 1.7 convolution_bitcast_fusion
  589.9 1.6 convolution_convert_fusion.2
  591.4 448.7 %all-reduce.2.cloned.1.call-done = f32[256,256]{0,1:T(8,128)} async-done(((f32[256,256]{0,1:T(8,128)}), f32[256,256]{0,1:T(8,128)}) %all-reduce.2.cloned.1.call-update) | async-done | bytes 262160 | tf_op jit(solution)/shard_map/psum | solution.py:99
  1040.1 1.0 constant_dynamic-slice_fusion
  1041.1 0.7 copy.12
  (25 shorter events, 0.3 us)
Async XLA Ops:
  7.2 0.9 copy-start
  7.2 66.4 %copy-start.6 = (s32[1,1,2,64]{3,2,1,0:T(2,128)S(1)}, s32[1,1,2,64]{3,2,1,0:T(2,128)}, u32[]{:S(2)}) copy-start(s32[1,1,2,64]{3,2,1,0:T(2,128)} %param.14) | copy-start | bytes 1540
  7.2 66.4 %copy-start.7 = (s32[1,1,2,64]{3,2,1,0:T(2,128)S(1)}, s32[1,1,2,64]{3,2,1,0:T(2,128)}, u32[]{:S(2)}) copy-start(s32[1,1,2,64]{3,2,1,0:T(2,128)} %param.13) | copy-start | bytes 1540
  7.2 286.2 %reduce-scatter.3.cloned.1.call-start = ((), (), s32[]{:S(2)}) async-start(), calls=%async_computation.2 | async-start | bytes 557056 | tf_op jit(solution)/shard_map/reduce_scatter | solution.py:66
  31.4 23.5 %collective-permute-start = (bf16[1024,256]{1,0:T(8,128)(2,1)S(1)}, bf16[1024,256]{1,0:T(8,128)(2,1)S(1)}, u32[]{:S(2)}, u32[]{:S(2)}) collective-permute-start(bf16[1024,256]{1,0:T(8,128)(2,1)S(1)} %all_gather.6), channel_id=1, source_target_pairs={{0,16},{16,32},{32,48},{48,64},{64,80},{80,96},{96,112},{112,128},... | collective-permute-start | bytes 1572872 | tf_op jit(solution)/shard_map/ppermute | solution.py:9
  33.5 68.3 %copy-start.4 = (s32[1,1,2]{2,1,0:T(1,128)S(1)}, s32[1,1,2]{2,1,0:T(1,128)}, u32[]{:S(2)}) copy-start(s32[1,1,2]{2,1,0:T(1,128)} %param.15) | copy-start | bytes 28
  54.9 16.7 %collective-permute-start.1 = (bf16[1024,256]{1,0:T(8,128)(2,1)S(1)}, bf16[1024,256]{1,0:T(8,128)(2,1)S(1)}, u32[]{:S(2)}, u32[]{:S(2)}) collective-permute-start(bf16[1024,256]{1,0:T(8,128)(2,1)S(1)} %broadcast_select_fusion), channel_id=1, source_target_pairs={{0,32},{16,48},{32,64},{48,80},{64,96},{80,112},{96,128},{112,144}... | collective-permute-start | bytes 1572872 | tf_op jit(solution)/shard_map/ppermute | solution.py:9
  71.7 27.6 %collective-permute-start.2 = (bf16[1024,256]{1,0:T(8,128)(2,1)S(1)}, bf16[1024,256]{1,0:T(8,128)(2,1)S(1)}, u32[]{:S(2)}, u32[]{:S(2)}) collective-permute-start(bf16[1024,256]{1,0:T(8,128)(2,1)S(1)} %broadcast_select_fusion.1), channel_id=1, source_target_pairs={{0,64},{16,80},{32,96},{48,112},{64,128},{80,144},{96,160},{112,17... | collective-permute-start | bytes 1572872 | tf_op jit(solution)/shard_map/ppermute | solution.py:9
  99.4 48.1 %collective-permute-start.3 = (bf16[1024,256]{1,0:T(8,128)(2,1)S(1)}, bf16[1024,256]{1,0:T(8,128)(2,1)S(1)}, u32[]{:S(2)}, u32[]{:S(2)}) collective-permute-start(bf16[1024,256]{1,0:T(8,128)(2,1)S(1)} %broadcast_select_fusion.2), channel_id=1, source_target_pairs={{0,128},{16,144},{32,160},{48,176},{64,192},{80,208},{96,224},{112... | collective-permute-start | bytes 1572872 | tf_op jit(solution)/shard_map/ppermute | solution.py:9
  147.5 33.9 %collective-permute-start.4 = (bf16[1024,256]{1,0:T(8,128)(2,1)S(1)}, bf16[1024,256]{1,0:T(8,128)(2,1)S(1)}, u32[]{:S(2)}, u32[]{:S(2)}) collective-permute-start(bf16[1024,256]{1,0:T(8,128)(2,1)S(1)} %broadcast_select_fusion.3), channel_id=1, source_target_pairs={{0,256},{16,272},{32,288},{48,304},{64,320},{80,336},{96,352},{112... | collective-permute-start | bytes 1572872 | tf_op jit(solution)/shard_map/ppermute | solution.py:9
  156.7 25.3 %copy-start.1 = (bf16[64,16384]{1,0:T(8,128)(2,1)}, bf16[64,16384]{1,0:T(8,128)(2,1)S(1)}, u32[]{:S(2)}) copy-start(bf16[64,16384]{1,0:T(8,128)(2,1)S(1)} %convolution_convert_fusion) | copy-start | bytes 6291460
  182.1 111.4 %copy-start.3 = (bf16[64,256]{1,0:T(8,128)(2,1)S(1)}, bf16[64,256]{1,0:T(8,128)(2,1)}, u32[]{:S(2)}) copy-start(bf16[64,256]{1,0:T(8,128)(2,1)} %param.11) | copy-start | bytes 98308
  182.1 111.3 %copy-start.5 = (f32[256]{0:T(256)S(1)}, f32[256]{0:T(256)}, u32[]{:S(2)}) copy-start(f32[256]{0:T(256)} %param.10) | copy-start | bytes 3076
  183.7 404.5 %reduce-scatter.5.cloned.1.call-start = ((), (), s32[]{:S(2)}) async-start(), calls=%async_computation.3 | async-start | bytes 557056 | tf_op jit(solution)/shard_map/reduce_scatter | solution.py:88
  318.7 38.6 %collective-permute-start.5 = (bf16[1024,256]{1,0:T(8,128)(2,1)S(1)}, bf16[1024,256]{1,0:T(8,128)(2,1)S(1)}, u32[]{:S(2)}, u32[]{:S(2)}) collective-permute-start(bf16[1024,256]{1,0:T(8,128)(2,1)S(1)} %fusion.19), channel_id=1, source_target_pairs={{0,256},{16,272},{32,288},{48,304},{64,320},{80,336},{96,352},{112... | collective-permute-start | bytes 1572872 | tf_op jit(solution)/shard_map/ppermute | solution.py:9
  358.0 40.2 %collective-permute-start.6 = (bf16[1024,256]{1,0:T(8,128)(2,1)S(1)}, bf16[1024,256]{1,0:T(8,128)(2,1)S(1)}, u32[]{:S(2)}, u32[]{:S(2)}) collective-permute-start(bf16[1024,256]{1,0:T(8,128)(2,1)S(1)} %get-tuple-element.17), channel_id=1, source_target_pairs={{0,384},{16,400},{32,416},{48,432},{64,448},{80,464},{96,480},{112... | collective-permute-start | bytes 1572872 | tf_op jit(solution)/shard_map/ppermute | solution.py:9
  398.4 51.6 %collective-permute-start.7 = (bf16[1024,256]{1,0:T(8,128)(2,1)S(1)}, bf16[1024,256]{1,0:T(8,128)(2,1)S(1)}, u32[]{:S(2)}, u32[]{:S(2)}) collective-permute-start(bf16[1024,256]{1,0:T(8,128)(2,1)S(1)} %convert_select_fusion.2), channel_id=1, source_target_pairs={{0,448},{16,464},{32,480},{48,496},{64,0},{80,16},{96,32},{112,48}... | collective-permute-start | bytes 1572872 | tf_op jit(solution)/shard_map/ppermute | solution.py:9
  450.2 15.7 %collective-permute-start.8 = (bf16[1024,256]{1,0:T(8,128)(2,1)S(1)}, bf16[1024,256]{1,0:T(8,128)(2,1)S(1)}, u32[]{:S(2)}, u32[]{:S(2)}) collective-permute-start(bf16[1024,256]{1,0:T(8,128)(2,1)S(1)} %fusion.26), channel_id=1, source_target_pairs={{0,480},{16,496},{32,0},{48,16},{64,32},{80,48},{96,64},{112,80},{... | collective-permute-start | bytes 1572872 | tf_op jit(solution)/shard_map/ppermute | solution.py:9
  466.1 122.1 %copy-start.2 = (bf16[64,256]{1,0:T(8,128)(2,1)S(1)}, bf16[64,256]{1,0:T(8,128)(2,1)}, u32[]{:S(2)}) copy-start(bf16[64,256]{1,0:T(8,128)(2,1)} %param.8) | copy-start | bytes 98308
  466.1 14.9 %collective-permute-start.9 = (bf16[1024,256]{1,0:T(8,128)(2,1)S(1)}, bf16[1024,256]{1,0:T(8,128)(2,1)S(1)}, u32[]{:S(2)}, u32[]{:S(2)}) collective-permute-start(bf16[1024,256]{1,0:T(8,128)(2,1)S(1)} %fusion.27), channel_id=1, source_target_pairs={{0,496},{16,0},{32,16},{48,32},{64,48},{80,64},{96,80},{112,96},{1... | collective-permute-start | bytes 1572872 | tf_op jit(solution)/shard_map/ppermute | solution.py:9
  482.1 558.0 %all-reduce.2.cloned.1.call-start = ((), (), s32[]{:S(2)}) async-start(), calls=%async_computation.4 | async-start | bytes 524288 | tf_op jit(solution)/shard_map/psum | solution.py:99
Sparse Core Ops, SparseCore 0:
  183.8 109.6 reduce-scatter.2
  482.2 85.5 reduce-scatter.4
  590.0 450.0 all-reduce.1
where the time goes:
time: 1050 us
  waiting for transfers between devices  787 us (75%)
  blocking collectives  150 us (14%)
  starting transfers between devices  74 us (7%)
  between operations  14.1 us (1%)
  matrix products  12.9 us (1%)
    psum x1, waiting for transfers between devices, body(): lax.psum((weight_terms, bias_terms), ('blk', 'rep'))  449 us
    ppermute x10, waiting for transfers between devices, passed_along(): lax.ppermute(x, axis, [(i, (i + by) % devices) for i in range(devices)])  229 us
    reduce_scatter x1, waiting for transfers between devices, body(): lax.psum_scatter(aggregate.astype(jnp.bfloat16), 'rep', scatter_dimension...  110 us
    psum x1, blocking collectives, body(): lax.psum((weight_terms, bias_terms), ('blk', 'rep'))  106 us
    ppermute x10, starting transfers between devices, passed_along(): lax.ppermute(x, axis, [(i, (i + by) % devices) for i in range(devices)])  73.9 us
    all_gather x1, blocking collectives, body(): feature_block = lax.all_gather(hw_slice, 'rep', axis=0, tiled=True)  22.4 us
    all_gather x1, blocking collectives, body(): grad_block = lax.all_gather(grad_rows, 'rep', axis=0, tiled=True)  21.4 us
  transfers between devices with their start and end apart: 13, of which 12 were waited for; matrix products, arithmetic and copies ran while one was open for 1% of the time, Pallas kernels for 0%

commit v1 on v0

--- a/solution.py
+++ b/solution.py
@@ -35,6 +35,12 @@
 
 
 def body(feats, weight, bias, grad_out, tile_values, tile_rows, tile_cols, tile_count):
+
+    def return_all_vectors(vector, link_axis, across):
+        for no in (link_axis, across):
+            vector = lax.psum(vector, no)
+        return vector
+
     replicas = lax.axis_size("rep")
     rep_index = lax.axis_index("rep")
     tile_size = tile_values.shape[-1]
@@ -96,7 +102,7 @@
     )
     weight_rows = weight.shape[0] // replicas
     bias_terms = jnp.sum(grad_rows.astype(jnp.float32), axis=0)
-    weight_total, grad_bias = lax.psum((weight_terms, bias_terms), ("blk", "rep"))
+    weight_total, grad_bias = return_all_vectors((weight_terms, bias_terms), "rep", "blk")
     grad_weight = lax.dynamic_slice_in_dim(weight_total, rep_index * weight_rows, weight_rows, 0)
     return (out, grad_feats, grad_weight, grad_bias)
 

time: 1050 us -> 998 us (0.950)
  the two profiles are of different devices: /device:TPU:4 before, /device:TPU:2 now
where the time goes in v1:
time: 998 us; the launch traced here: 997 us
  waiting for transfers between devices  737 us (74%)
  blocking collectives  146 us (15%)
  starting transfers between devices  77.3 us (8%)
  between operations  14.1 us (1%)
  matrix products  12.9 us (1%)
    psum x2, waiting for transfers between devices, return_all_vectors(): vector = lax.psum(vector, no)  316 us
    ppermute x10, waiting for transfers between devices, passed_along(): lax.ppermute(x, axis, [(i, (i + by) % devices) for i in range(devices)])  237 us
    psum x2, blocking collectives, return_all_vectors(): vector = lax.psum(vector, no)  101 us
    reduce_scatter x1, waiting for transfers between devices, body(): lax.psum_scatter(aggregate.astype(jnp.bfloat16), 'rep', scatter_dimension...  97.9 us
    reduce_scatter x1, waiting for transfers between devices, body(): lax.psum_scatter(partial_grad.astype(jnp.bfloat16), 'rep', scatter_dimens...  85.5 us
    ppermute x10, starting transfers between devices, passed_along(): lax.ppermute(x, axis, [(i, (i + by) % devices) for i in range(devices)])  77.1 us
    all_gather x1, blocking collectives, body(): feature_block = lax.all_gather(hw_slice, 'rep', axis=0, tiled=True)  23.8 us
    all_gather x1, blocking collectives, body(): grad_block = lax.all_gather(grad_rows, 'rep', axis=0, tiled=True)  21.2 us
  transfers between devices with their start and end apart: 14, of which 14 were waited for; matrix products, arithmetic and copies ran while one was open for 1% of the time, Pallas kernels for 0%

profile of v1, /device:TPU:2, one launch (start us, length us, event | category | flops | bytes accessed | tf_op | source)
XLA Modules:
  0.0 997.0 jit_solution(9610833215569753904)
XLA Ops:
  7.2 0.8 copy-done
  8.1 0.9 convolution_convert_fusion.3
  9.0 23.8 %all_gather.6 = bf16[1024,256]{1,0:T(8,128)(2,1)S(1)} all-gather(bf16[64,256]{1,0:T(8,128)(2,1)S(1)} %convolution_convert_fusion.3), channel_id=1, replica_groups=mesh['blk'=32,'rep'=16] {'rep'}, dimensions={0}, use_global_device_ids=true | all-gather | bytes 557056 | tf_op jit(solution)/shard_map/all_gather | solution.py:54
  32.7 2.5 collective-permute-start
  35.3 21.3 %collective-permute-done = bf16[1024,256]{1,0:T(8,128)(2,1)S(1)} collective-permute-done((bf16[1024,256]{1,0:T(8,128)(2,1)S(1)}, bf16[1024,256]{1,0:T(8,128)(2,1)S(1)}, u32[]{:S(2)}, u32[]{:S(2)}) %collective-permute-start) | collective-permute-done | bytes 524320 | tf_op jit(solution)/shard_map/ppermute | solution.py:9
  56.7 1.9 collective-permute-start.1
  58.6 14.7 %collective-permute-done.1 = bf16[1024,256]{1,0:T(8,128)(2,1)S(1)} collective-permute-done((bf16[1024,256]{1,0:T(8,128)(2,1)S(1)}, bf16[1024,256]{1,0:T(8,128)(2,1)S(1)}, u32[]{:S(2)}, u32[]{:S(2)}) %collective-permute-start.1) | collective-permute-done | bytes 524320 | tf_op jit(solution)/shard_map/ppermute | solution.py:9
  73.4 1.9 collective-permute-start.2
  75.4 25.2 %collective-permute-done.2 = bf16[1024,256]{1,0:T(8,128)(2,1)S(1)} collective-permute-done((bf16[1024,256]{1,0:T(8,128)(2,1)S(1)}, bf16[1024,256]{1,0:T(8,128)(2,1)S(1)}, u32[]{:S(2)}, u32[]{:S(2)}) %collective-permute-start.2) | collective-permute-done | bytes 524320 | tf_op jit(solution)/shard_map/ppermute | solution.py:9
  100.7 2.9 collective-permute-start.3
  103.7 0.6 fusion.37
  104.2 0.6 iota_compare_fusion.3
  104.9 2.7 fusion.36
  107.6 39.3 %collective-permute-done.3 = bf16[1024,256]{1,0:T(8,128)(2,1)S(1)} collective-permute-done((bf16[1024,256]{1,0:T(8,128)(2,1)S(1)}, bf16[1024,256]{1,0:T(8,128)(2,1)S(1)}, u32[]{:S(2)}, u32[]{:S(2)}) %collective-permute-start.3) | collective-permute-done | bytes 524320 | tf_op jit(solution)/shard_map/ppermute | solution.py:9
  147.0 5.7 collective-permute-start.4
  152.7 1.7 convolution_convert_fusion.1
  154.4 0.7 iota_compare_fusion.2
  155.1 1.7 convolution_convert_fusion
  156.8 37.7 %collective-permute-done.4 = bf16[1024,256]{1,0:T(8,128)(2,1)S(1)} collective-permute-done((bf16[1024,256]{1,0:T(8,128)(2,1)S(1)}, bf16[1024,256]{1,0:T(8,128)(2,1)S(1)}, u32[]{:S(2)}, u32[]{:S(2)}) %collective-permute-start.4) | collective-permute-done | bytes 524320 | tf_op jit(solution)/shard_map/ppermute | solution.py:9
  194.5 0.7 fusion.2
  195.2 1.5 fusion.22
  196.8 97.9 %reduce-scatter.3.cloned.1.call-done = bf16[64,256]{1,0:T(8,128)(2,1)} async-done(((bf16[1024,256]{1,0:T(8,128)(2,1)}), bf16[64,256]{1,0:T(8,128)(2,1)}) %reduce-scatter.3.cloned.1.call-update) | async-done | bytes 32784 | tf_op jit(solution)/shard_map/reduce_scatter | solution.py:72
  294.7 1.4 convert_reduce_fusion
  296.1 21.2 %all_gather.7 = bf16[1024,256]{1,0:T(8,128)(2,1)S(1)} all-gather(bf16[64,256]{1,0:T(8,128)(2,1)S(1)} %get-tuple-element.9), channel_id=1, replica_groups=mesh['blk'=32,'rep'=16] {'rep'}, dimensions={0}, use_global_device_ids=true | all-gather | bytes 557056 | tf_op jit(solution)/shard_map/all_gather | solution.py:76
  317.3 2.4 fusion.19
  319.7 12.8 %collective-permute-start.5 = (bf16[1024,256]{1,0:T(8,128)(2,1)S(1)}, bf16[1024,256]{1,0:T(8,128)(2,1)S(1)}, u32[]{:S(2)}, u32[]{:S(2)}) collective-permute-start(bf16[1024,256]{1,0:T(8,128)(2,1)S(1)} %fusion.19), channel_id=1, source_target_pairs={{0,256},{16,272},{32,288},{48,304},{64,320},{80,336},{96,352},{112... | collective-permute-start | bytes 1572872 | tf_op jit(solution)/shard_map/ppermute | solution.py:9
  332.4 25.8 %collective-permute-done.5 = bf16[1024,256]{1,0:T(8,128)(2,1)S(1)} collective-permute-done((bf16[1024,256]{1,0:T(8,128)(2,1)S(1)}, bf16[1024,256]{1,0:T(8,128)(2,1)S(1)}, u32[]{:S(2)}, u32[]{:S(2)}) %collective-permute-start.5) | collective-permute-done | bytes 524320 | tf_op jit(solution)/shard_map/ppermute | solution.py:9
  358.2 0.8 fusion.25
  359.0 17.2 %collective-permute-start.6 = (bf16[1024,256]{1,0:T(8,128)(2,1)S(1)}, bf16[1024,256]{1,0:T(8,128)(2,1)S(1)}, u32[]{:S(2)}, u32[]{:S(2)}) collective-permute-start(bf16[1024,256]{1,0:T(8,128)(2,1)S(1)} %get-tuple-element.17), channel_id=1, source_target_pairs={{0,384},{16,400},{32,416},{48,432},{64,448},{80,464},{96,480},{112... | collective-permute-start | bytes 1572872 | tf_op jit(solution)/shard_map/ppermute | solution.py:9
  376.2 23.5 %collective-permute-done.6 = bf16[1024,256]{1,0:T(8,128)(2,1)S(1)} collective-permute-done((bf16[1024,256]{1,0:T(8,128)(2,1)S(1)}, bf16[1024,256]{1,0:T(8,128)(2,1)S(1)}, u32[]{:S(2)}, u32[]{:S(2)}) %collective-permute-start.6) | collective-permute-done | bytes 524320 | tf_op jit(solution)/shard_map/ppermute | solution.py:9
  399.7 0.2 convert_select_fusion.2
  399.9 26.3 %collective-permute-start.7 = (bf16[1024,256]{1,0:T(8,128)(2,1)S(1)}, bf16[1024,256]{1,0:T(8,128)(2,1)S(1)}, u32[]{:S(2)}, u32[]{:S(2)}) collective-permute-start(bf16[1024,256]{1,0:T(8,128)(2,1)S(1)} %convert_select_fusion.2), channel_id=1, source_target_pairs={{0,448},{16,464},{32,480},{48,496},{64,0},{80,16},{96,32},{112,48}... | collective-permute-start | bytes 1572872 | tf_op jit(solution)/shard_map/ppermute | solution.py:9
  426.2 24.9 %collective-permute-done.7 = bf16[1024,256]{1,0:T(8,128)(2,1)S(1)} collective-permute-done((bf16[1024,256]{1,0:T(8,128)(2,1)S(1)}, bf16[1024,256]{1,0:T(8,128)(2,1)S(1)}, u32[]{:S(2)}, u32[]{:S(2)}) %collective-permute-start.7) | collective-permute-done | bytes 524320 | tf_op jit(solution)/shard_map/ppermute | solution.py:9
  451.2 1.9 collective-permute-start.8
  453.1 13.8 %collective-permute-done.8 = bf16[1024,256]{1,0:T(8,128)(2,1)S(1)} collective-permute-done((bf16[1024,256]{1,0:T(8,128)(2,1)S(1)}, bf16[1024,256]{1,0:T(8,128)(2,1)S(1)}, u32[]{:S(2)}, u32[]{:S(2)}) %collective-permute-start.8) | collective-permute-done | bytes 524320 | tf_op jit(solution)/shard_map/ppermute | solution.py:9
  466.9 0.2 fusion.27
  467.1 4.0 collective-permute-start.9
  471.1 10.9 %collective-permute-done.9 = bf16[1024,256]{1,0:T(8,128)(2,1)S(1)} collective-permute-done((bf16[1024,256]{1,0:T(8,128)(2,1)S(1)}, bf16[1024,256]{1,0:T(8,128)(2,1)S(1)}, u32[]{:S(2)}, u32[]{:S(2)}) %collective-permute-start.9) | collective-permute-done | bytes 524320 | tf_op jit(solution)/shard_map/ppermute | solution.py:9
  482.0 1.0 select_convert_fusion
  483.1 85.5 %reduce-scatter.5.cloned.1.call-done = bf16[64,256]{1,0:T(8,128)(2,1)} async-done(((bf16[1024,256]{1,0:T(8,128)(2,1)}), bf16[64,256]{1,0:T(8,128)(2,1)}) %reduce-scatter.5.cloned.1.call-update) | async-done | bytes 32784 | tf_op jit(solution)/shard_map/reduce_scatter | solution.py:94
  568.6 1.7 convolution_bitcast_fusion
  570.4 147.3 %all-reduce.3.cloned.1.call-done = f32[256,256]{0,1:T(8,128)} async-done(((f32[256,256]{0,1:T(8,128)}), f32[256,256]{0,1:T(8,128)}) %all-reduce.3.cloned.1.call-update) | async-done | bytes 262160 | tf_op jit(solution)/shard_map/psum | solution.py:41
  717.6 36.2 %psum.30 = f32[256]{0:T(256)S(1)} all-reduce(f32[256]{0:T(256)S(1)} %get-tuple-element.8), channel_id=1, replica_groups=mesh['blk'=32,'rep'=16] {'rep'}, use_global_device_ids=true, to_apply=%region_5.6 | all-reduce | flops 256 | bytes 2048 | tf_op jit(solution)/shard_map/psum | solution.py:41
  753.8 64.6 %psum.31 = f32[256]{0:T(256)} all-reduce(f32[256]{0:T(256)S(1)} %psum.30), channel_id=1, replica_groups=mesh['blk'=32,'rep'=16] {'blk'}, use_global_device_ids=true, to_apply=%region_6.7 | all-reduce | flops 256 | bytes 2048 | tf_op jit(solution)/shard_map/psum | solution.py:41
  818.4 1.6 convolution_convert_fusion.2
  819.9 168.8 %all-reduce.5.cloned.1.call-done = f32[256,256]{0,1:T(8,128)} async-done(((f32[256,256]{0,1:T(8,128)}), f32[256,256]{0,1:T(8,128)}) %all-reduce.5.cloned.1.call-update) | async-done | bytes 262160 | tf_op jit(solution)/shard_map/psum | solution.py:41
  988.8 1.0 constant_dynamic-slice_fusion
  989.8 0.7 copy.12
  (29 shorter events, 0.6 us)
Async XLA Ops:
  7.2 0.9 copy-start
  7.2 68.2 %copy-start.6 = (s32[1,1,2,64]{3,2,1,0:T(2,128)S(1)}, s32[1,1,2,64]{3,2,1,0:T(2,128)}, u32[]{:S(2)}) copy-start(s32[1,1,2,64]{3,2,1,0:T(2,128)} %param.14) | copy-start | bytes 1540
  7.2 68.2 %copy-start.7 = (s32[1,1,2,64]{3,2,1,0:T(2,128)S(1)}, s32[1,1,2,64]{3,2,1,0:T(2,128)}, u32[]{:S(2)}) copy-start(s32[1,1,2,64]{3,2,1,0:T(2,128)} %param.13) | copy-start | bytes 1540
  7.2 287.5 %reduce-scatter.3.cloned.1.call-start = ((), (), s32[]{:S(2)}) async-start(), calls=%async_computation.2 | async-start | bytes 557056 | tf_op jit(solution)/shard_map/reduce_scatter | solution.py:72
  32.7 23.9 %collective-permute-start = (bf16[1024,256]{1,0:T(8,128)(2,1)S(1)}, bf16[1024,256]{1,0:T(8,128)(2,1)S(1)}, u32[]{:S(2)}, u32[]{:S(2)}) collective-permute-start(bf16[1024,256]{1,0:T(8,128)(2,1)S(1)} %all_gather.6), channel_id=1, source_target_pairs={{0,16},{16,32},{32,48},{48,64},{64,80},{80,96},{96,112},{112,128},... | collective-permute-start | bytes 1572872 | tf_op jit(solution)/shard_map/ppermute | solution.py:9
  35.3 68.4 %copy-start.4 = (s32[1,1,2]{2,1,0:T(1,128)S(1)}, s32[1,1,2]{2,1,0:T(1,128)}, u32[]{:S(2)}) copy-start(s32[1,1,2]{2,1,0:T(1,128)} %param.15) | copy-start | bytes 28
  56.7 16.7 %collective-permute-start.1 = (bf16[1024,256]{1,0:T(8,128)(2,1)S(1)}, bf16[1024,256]{1,0:T(8,128)(2,1)S(1)}, u32[]{:S(2)}, u32[]{:S(2)}) collective-permute-start(bf16[1024,256]{1,0:T(8,128)(2,1)S(1)} %broadcast_select_fusion), channel_id=1, source_target_pairs={{0,32},{16,48},{32,64},{48,80},{64,96},{80,112},{96,128},{112,144}... | collective-permute-start | bytes 1572872 | tf_op jit(solution)/shard_map/ppermute | solution.py:9
  73.4 27.2 %collective-permute-start.2 = (bf16[1024,256]{1,0:T(8,128)(2,1)S(1)}, bf16[1024,256]{1,0:T(8,128)(2,1)S(1)}, u32[]{:S(2)}, u32[]{:S(2)}) collective-permute-start(bf16[1024,256]{1,0:T(8,128)(2,1)S(1)} %broadcast_select_fusion.1), channel_id=1, source_target_pairs={{0,64},{16,80},{32,96},{48,112},{64,128},{80,144},{96,160},{112,17... | collective-permute-start | bytes 1572872 | tf_op jit(solution)/shard_map/ppermute | solution.py:9
  100.7 46.3 %collective-permute-start.3 = (bf16[1024,256]{1,0:T(8,128)(2,1)S(1)}, bf16[1024,256]{1,0:T(8,128)(2,1)S(1)}, u32[]{:S(2)}, u32[]{:S(2)}) collective-permute-start(bf16[1024,256]{1,0:T(8,128)(2,1)S(1)} %broadcast_select_fusion.2), channel_id=1, source_target_pairs={{0,128},{16,144},{32,160},{48,176},{64,192},{80,208},{96,224},{112... | collective-permute-start | bytes 1572872 | tf_op jit(solution)/shard_map/ppermute | solution.py:9
  147.0 47.4 %collective-permute-start.4 = (bf16[1024,256]{1,0:T(8,128)(2,1)S(1)}, bf16[1024,256]{1,0:T(8,128)(2,1)S(1)}, u32[]{:S(2)}, u32[]{:S(2)}) collective-permute-start(bf16[1024,256]{1,0:T(8,128)(2,1)S(1)} %broadcast_select_fusion.3), channel_id=1, source_target_pairs={{0,256},{16,272},{32,288},{48,304},{64,320},{80,336},{96,352},{112... | collective-permute-start | bytes 1572872 | tf_op jit(solution)/shard_map/ppermute | solution.py:9
  156.8 38.4 %copy-start.1 = (bf16[64,16384]{1,0:T(8,128)(2,1)}, bf16[64,16384]{1,0:T(8,128)(2,1)S(1)}, u32[]{:S(2)}) copy-start(bf16[64,16384]{1,0:T(8,128)(2,1)S(1)} %convolution_convert_fusion) | copy-start | bytes 6291460
  195.2 99.5 %copy-start.3 = (bf16[64,256]{1,0:T(8,128)(2,1)S(1)}, bf16[64,256]{1,0:T(8,128)(2,1)}, u32[]{:S(2)}) copy-start(bf16[64,256]{1,0:T(8,128)(2,1)} %param.11) | copy-start | bytes 98308
  195.2 99.5 %copy-start.5 = (f32[256]{0:T(256)S(1)}, f32[256]{0:T(256)}, u32[]{:S(2)}) copy-start(f32[256]{0:T(256)} %param.10) | copy-start | bytes 3076
  196.8 371.9 %reduce-scatter.5.cloned.1.call-start = ((), (), s32[]{:S(2)}) async-start(), calls=%async_computation.3 | async-start | bytes 557056 | tf_op jit(solution)/shard_map/reduce_scatter | solution.py:94
  319.7 38.6 %collective-permute-start.5 = (bf16[1024,256]{1,0:T(8,128)(2,1)S(1)}, bf16[1024,256]{1,0:T(8,128)(2,1)S(1)}, u32[]{:S(2)}, u32[]{:S(2)}) collective-permute-start(bf16[1024,256]{1,0:T(8,128)(2,1)S(1)} %fusion.19), channel_id=1, source_target_pairs={{0,256},{16,272},{32,288},{48,304},{64,320},{80,336},{96,352},{112... | collective-permute-start | bytes 1572872 | tf_op jit(solution)/shard_map/ppermute | solution.py:9
  359.0 40.7 %collective-permute-start.6 = (bf16[1024,256]{1,0:T(8,128)(2,1)S(1)}, bf16[1024,256]{1,0:T(8,128)(2,1)S(1)}, u32[]{:S(2)}, u32[]{:S(2)}) collective-permute-start(bf16[1024,256]{1,0:T(8,128)(2,1)S(1)} %get-tuple-element.17), channel_id=1, source_target_pairs={{0,384},{16,400},{32,416},{48,432},{64,448},{80,464},{96,480},{112... | collective-permute-start | bytes 1572872 | tf_op jit(solution)/shard_map/ppermute | solution.py:9
  399.9 51.2 %collective-permute-start.7 = (bf16[1024,256]{1,0:T(8,128)(2,1)S(1)}, bf16[1024,256]{1,0:T(8,128)(2,1)S(1)}, u32[]{:S(2)}, u32[]{:S(2)}) collective-permute-start(bf16[1024,256]{1,0:T(8,128)(2,1)S(1)} %convert_select_fusion.2), channel_id=1, source_target_pairs={{0,448},{16,464},{32,480},{48,496},{64,0},{80,16},{96,32},{112,48}... | collective-permute-start | bytes 1572872 | tf_op jit(solution)/shard_map/ppermute | solution.py:9
  451.2 15.7 %collective-permute-start.8 = (bf16[1024,256]{1,0:T(8,128)(2,1)S(1)}, bf16[1024,256]{1,0:T(8,128)(2,1)S(1)}, u32[]{:S(2)}, u32[]{:S(2)}) collective-permute-start(bf16[1024,256]{1,0:T(8,128)(2,1)S(1)} %fusion.26), channel_id=1, source_target_pairs={{0,480},{16,496},{32,0},{48,16},{64,32},{80,48},{96,64},{112,80},{... | collective-permute-start | bytes 1572872 | tf_op jit(solution)/shard_map/ppermute | solution.py:9
  467.1 101.5 %copy-start.2 = (bf16[64,256]{1,0:T(8,128)(2,1)S(1)}, bf16[64,256]{1,0:T(8,128)(2,1)}, u32[]{:S(2)}) copy-start(bf16[64,256]{1,0:T(8,128)(2,1)} %param.8) | copy-start | bytes 98308
  467.1 14.9 %collective-permute-start.9 = (bf16[1024,256]{1,0:T(8,128)(2,1)S(1)}, bf16[1024,256]{1,0:T(8,128)(2,1)S(1)}, u32[]{:S(2)}, u32[]{:S(2)}) collective-permute-start(bf16[1024,256]{1,0:T(8,128)(2,1)S(1)} %fusion.27), channel_id=1, source_target_pairs={{0,496},{16,0},{32,16},{48,32},{64,48},{80,64},{96,80},{112,96},{1... | collective-permute-start | bytes 1572872 | tf_op jit(solution)/shard_map/ppermute | solution.py:9
  483.1 234.6 %all-reduce.3.cloned.1.call-start = ((), (), s32[]{:S(2)}) async-start(), calls=%async_computation.4 | async-start | bytes 524288 | tf_op jit(solution)/shard_map/psum | solution.py:41
  570.3 418.5 %all-reduce.5.cloned.1.call-start = ((), (), s32[]{:S(2)}) async-start(), calls=%async_computation.5 | async-start | bytes 524288 | tf_op jit(solution)/shard_map/psum | solution.py:41
Sparse Core Ops, SparseCore 0:
  196.9 97.7 reduce-scatter.2
  483.2 85.3 reduce-scatter.4
  571.5 146.0 all-reduce.2
  720.6 268.0 all-reduce.4
